TPU v7x, 32 devices: a whole 2x2x4 slice. The times are simulated.
32 devices in a mesh: groups: 2 (over y), pts: 4 (over z), cam: 4 (over x, core).
Axes of the slice: x: 2, y: 2, z: 4, core: 2. Of those that a mesh axis runs over, the one named last changes fastest.
Arguments:
- cam_jac: float32 [2, 9, 131072], P(None, None, ('groups', 'pts', 'cam')), parts along dimension 2, may hold values from -0.4 to 0.4
- point_jac: float32 [2, 3, 131072], P(None, None, ('groups', 'pts', 'cam')), parts along dimension 2, may hold values from -3 to 3
- obs_cam: int32 [131072], P(('groups', 'pts', 'cam')), parts along dimension 0, may hold values from 0 to 511
- obs_point: int32 [131072], P(('groups', 'pts', 'cam')), parts along dimension 0, may hold values from 0 to 4095
- point_damp: float32 [32768], P(('groups', 'pts')), parts along dimension 0, may hold values from 0.5 to 4
- cam_damp: float32 [4096], P(('groups', 'cam')), parts along dimension 0, may hold values from 0.5 to 4
- reduced_rhs: float32 [9, 4096], P(None, ('groups', 'cam')), parts along dimension 1, may hold values from -6 to 6
Outputs:
- solution: float32 [9, 4096], P(None, ('groups', 'cam')), parts along dimension 1
- residual: float32 [9, 4096], P(None, ('groups', 'cam')), parts along dimension 1
There are 2 independent parts, one for each index of `groups`. A program takes and returns all parts, laid end to end along the dimension named above; each array names one. Nothing has to cross between parts.
All inputs are finite; a program needn't handle non-finite values.
Results may differ from a plain program's by a relative error of at most 0.0003.
Values sent between devices are 32-bit elements; how exact they have to be, the bound alone decides.
No kernel may reach another device: no remote copies, remote signals or barrier semaphores. Data moves between devices by JAX's collectives and lax.ppermute only.
A program may use at most 64 MiB of HBM per device.

v0:
```python
import jax
import jax.numpy as jnp
from jax import lax
from jax.sharding import PartitionSpec as P

ITERS = 3
BF = jnp.bfloat16
F32 = jnp.float32


def split_of(count):
    lo = 1 << max(count.bit_length() - 1, 0) // 2
    while count % lo:
        lo //= 2
    return (count // lo, lo)


def pieces(value):
    first = lax.reduce_precision(value, exponent_bits=8, mantissa_bits=7)
    rest = value - first
    second = lax.reduce_precision(rest, exponent_bits=8, mantissa_bits=7)
    third = rest - second
    return (first.astype(BF), second.astype(BF), third.astype(BF))


class Index:

    def __init__(self, index, count):
        self.count = count
        self.hi, self.lo = split_of(count)
        high = index // self.lo
        low = index % self.lo
        hot = lax.broadcasted_iota(jnp.int32, (self.hi, index.shape[0]), 0) == high[None, :]
        self.hot = hot.astype(BF)
        self.hot3 = jnp.concatenate([self.hot] * 3, axis=1)
        self.hot3t = jnp.concatenate([self.hot] * 3, axis=0)
        self.low = lax.broadcasted_iota(jnp.int32, (self.lo, index.shape[0]), 0) == low[None, :]

    def segsum(self, terms):
        ncol = terms.shape[0]
        parts = [
            jnp.where(self.low[None], part[:, None, :], jnp.zeros((), BF)).reshape(
                ncol * self.lo, -1
            )
            for part in pieces(terms)
        ]
        spread = jnp.concatenate(parts, axis=1)
        out = lax.dot_general(
            self.hot3, spread, (((1,), (1,)), ((), ())), preferred_element_type=F32
        )
        return out.reshape(self.hi, ncol, self.lo).transpose(1, 0, 2).reshape(ncol, self.count)

    def gather(self, table):
        ncol = table.shape[0]
        mat = (
            table.reshape(ncol, self.hi, self.lo)
            .transpose(0, 2, 1)
            .reshape(ncol * self.lo, self.hi)
        )
        stacked = jnp.concatenate(pieces(mat), axis=1)
        spread = lax.dot_general(
            stacked, self.hot3t, (((1,), (0,)), ((), ())), preferred_element_type=F32
        ).reshape(ncol, self.lo, -1)
        return jnp.sum(jnp.where(self.low[None], spread, 0.0), axis=1)


def invert3(mat):
    c00 = mat[1, 1] * mat[2, 2] - mat[1, 2] * mat[2, 1]
    c01 = mat[0, 2] * mat[2, 1] - mat[0, 1] * mat[2, 2]
    c02 = mat[0, 1] * mat[1, 2] - mat[0, 2] * mat[1, 1]
    c10 = mat[1, 2] * mat[2, 0] - mat[1, 0] * mat[2, 2]
    c11 = mat[0, 0] * mat[2, 2] - mat[0, 2] * mat[2, 0]
    c12 = mat[0, 2] * mat[1, 0] - mat[0, 0] * mat[1, 2]
    c20 = mat[1, 0] * mat[2, 1] - mat[1, 1] * mat[2, 0]
    c21 = mat[0, 1] * mat[2, 0] - mat[0, 0] * mat[2, 1]
    c22 = mat[0, 0] * mat[1, 1] - mat[0, 1] * mat[1, 0]
    det = mat[0, 0] * c00 + mat[0, 1] * c10 + mat[0, 2] * c20
    adj = jnp.stack(
        [jnp.stack([c00, c01, c02]), jnp.stack([c10, c11, c12]), jnp.stack([c20, c21, c22])]
    )
    return adj / det


def normal_six(point_jac):
    pairs = [(0, 0), (0, 1), (0, 2), (1, 1), (1, 2), (2, 2)]
    return jnp.stack(
        [jnp.sum(point_jac[:, first] * point_jac[:, second], axis=0) for first, second in pairs]
    )


def expand_six(six):
    return jnp.stack(
        [
            jnp.stack([six[0], six[1], six[2]]),
            jnp.stack([six[1], six[3], six[4]]),
            jnp.stack([six[2], six[4], six[5]]),
        ]
    )


def point_inverse(six, damp):
    mat = expand_six(six) + damp[None, None, :] * jnp.eye(3, dtype=jnp.float32)[:, :, None]
    return invert3(mat)


def norm_sum(value):
    return lax.psum(value, "cam")


def on_device(cam_jac, point_jac, obs_cam, obs_point, point_damp, cam_damp, reduced_rhs):
    npts = point_damp.shape[0]
    ncam = reduced_rhs.shape[1]
    by_point = Index(obs_point, npts)
    by_cam = Index(obs_cam, ncam)
    six_terms = by_point.segsum(normal_six(point_jac))
    pshare = npts // lax.axis_size("cam")
    pstart = lax.axis_index("cam") * pshare
    six_share = lax.psum_scatter(six_terms, "cam", scatter_dimension=1, tiled=True)
    damp_pts = lax.dynamic_slice_in_dim(point_damp, pstart, pshare, 0)
    inv_share = point_inverse(six_share, damp_pts)
    diag_terms = by_cam.segsum(jnp.sum(cam_jac * cam_jac, axis=0))
    cam_diag = lax.psum(diag_terms, "pts") + cam_damp[None, :]
    solution = jnp.zeros_like(reduced_rhs)
    residual = reduced_rhs
    pre = residual / cam_diag
    direction = pre
    rz = norm_sum(jnp.sum(residual * pre))
    for step in range(ITERS):
        dir_obs = by_cam.gather(direction)
        y = jnp.sum(cam_jac * dir_obs[None], axis=1)
        reduced_u_part = by_point.segsum(jnp.sum(point_jac * y[:, None, :], axis=0))
        u_share = lax.psum_scatter(reduced_u_part, "cam", scatter_dimension=1, tiled=True)
        w_share = jnp.sum(inv_share * u_share[None, :, :], axis=1)
        w = lax.all_gather(w_share, "cam", axis=1, tiled=True)
        z = y - jnp.sum(point_jac * by_point.gather(w)[None], axis=1)
        image = cam_damp[None, :] * direction + lax.psum(
            by_cam.segsum(jnp.sum(cam_jac * z[:, None, :], axis=0)), "pts"
        )
        alpha = rz / lax.psum(jnp.sum(direction * image), "cam")
        solution = solution + alpha * direction
        residual = residual - alpha * image
        pre = residual / cam_diag
        new_rz = norm_sum(jnp.sum(residual * pre))
        direction = pre + new_rz / rz * direction
        rz = new_rz
    return (solution, residual)


def solution(mesh):
    return jax.shard_map(
        on_device,
        mesh=mesh,
        in_specs=(
            P(None, None, ("groups", "pts", "cam")),
            P(None, None, ("groups", "pts", "cam")),
            P(("groups", "pts", "cam")),
            P(("groups", "pts", "cam")),
            P(("groups", "pts")),
            P(("groups", "cam")),
            P(None, ("groups", "cam")),
        ),
        out_specs=(P(None, ("groups", "cam")), P(None, ("groups", "cam"))),
        check_vma=False,
    )
```

profile of v0, /device:TPU:0, one launch (start us, length us, event | category | flops | bytes accessed | tf_op | source)
XLA Modules:
  0.0 301.3 jit_solution(13803809787770061255)
XLA Ops:
  8.7 1.4 multiply_reduce_fusion.6
  10.6 1.1 fusion.24
  12.0 20.9 %psum.70 = f32[9,512]{1,0:T(8,128)S(1)} all-reduce(f32[9,512]{1,0:T(8,128)S(1)} %reshape.948), channel_id=1, replica_groups=mesh['groups'=2,'pts'=4,'cam'=4] {'pts'}, use_global_device_ids=true, to_apply=%region_1.2 | all-reduce | flops 4608 | bytes 36864 | tf_op jit(solution)/shard_map/psum | solution.py:122
  35.6 1.4 fusion.6
  37.1 2.9 copy.107
  40.5 0.9 broadcast_select_fusion.2
  41.4 3.0 %fusion = f32[64,384]{1,0:T(8,128)S(1)} fusion(bf16[384,4096]{1,0:T(8,128)(2,1)S(1)} %bitcast.157, bf16[384,4096]{1,0:T(8,128)(2,1)S(1)} %bitcast.156, bf16[384,4096]{1,0:T(8,128)(2,1)S(1)} %bitcast.155, bf16[64,4096]{1,0:T(8,128)(2,1)S(1)} %get-tuple-element.105), kind=kOutput, calls=%fused_computation | convolution fusion | flops 637009920 | bytes 10059776 | tf_op jit(solution)/shard_map/dot_general | solution.py:48
  46.2 23.4 %reduce-scatter.13.cloned.1.call-done = f32[1024,3]{1,0:T(8,128)} async-done(((f32[4096,3]{1,0:T(8,128)}), f32[1024,3]{1,0:T(8,128)}) %reduce-scatter.13.cloned.1.call-update) | async-done | bytes 12304
  69.5 1.2 copy.102
  70.8 20.9 %reduce-scatter.11.cloned.1.call-done = f32[6,1024]{1,0:T(8,128)} async-done(((f32[6,4096]{1,0:T(8,128)}), f32[6,1024]{1,0:T(8,128)}) %reduce-scatter.11.cloned.1.call-update) | async-done | bytes 24592 | tf_op jit(solution)/shard_map/reduce_scatter | solution.py:118
  94.4 5.4 %all_gather.9 = f32[3,4096]{1,0:T(4,128)S(1)} all-gather(f32[3,1024]{1,0:T(4,128)S(1)} %get-tuple-element.16), channel_id=1, replica_groups=mesh['groups'=2,'pts'=4,'cam'=4] {'cam'}, dimensions={1}, use_global_device_ids=true | all-gather | bytes 61440 | tf_op jit(solution)/shard_map/all_gather | solution.py:134
  102.1 1.1 fusion.30
  103.4 19.0 %psum.72 = f32[9,512]{1,0:T(8,128)S(1)} all-reduce(f32[9,512]{1,0:T(8,128)S(1)} %reshape.960), channel_id=1, replica_groups=mesh['groups'=2,'pts'=4,'cam'=4] {'pts'}, use_global_device_ids=true, to_apply=%region_19.20 | all-reduce | flops 4608 | bytes 36864 | tf_op jit(solution)/shard_map/psum | solution.py:136
  123.0 6.6 %all-reduce = (f32[]{:T(128)}, f32[]{:T(128)}) all-reduce(f32[]{:T(128)} %get-tuple-element.9, f32[]{:T(128)} %get-tuple-element.8), channel_id=1, replica_groups=mesh['groups'=2,'pts'=4,'cam'=4] {'cam'}, use_global_device_ids=true, to_apply=%region_3.4 | all-reduce | flops 2 | bytes 16 | tf_op jit(solution)/shard_map/psum | solution.py:107
  131.6 6.4 %psum.74 = f32[]{:T(128)} all-reduce(f32[]{:T(128)} %get-tuple-element.14), channel_id=1, replica_groups=mesh['groups'=2,'pts'=4,'cam'=4] {'cam'}, use_global_device_ids=true, to_apply=%region_23.24 | all-reduce | flops 1 | bytes 8 | tf_op jit(solution)/shard_map/psum | solution.py:107
  141.3 1.4 fusion.12
  142.8 2.9 copy.108
  145.8 29.0 %reduce-scatter.15.cloned.1.call-done = f32[1024,3]{1,0:T(8,128)} async-done(((f32[4096,3]{1,0:T(8,128)}), f32[1024,3]{1,0:T(8,128)}) %reduce-scatter.15.cloned.1.call-update) | async-done | bytes 12304
  174.8 1.2 copy.104
  176.1 5.2 %all_gather.10 = f32[3,4096]{1,0:T(4,128)S(1)} all-gather(f32[3,1024]{1,0:T(4,128)S(1)} %multiply_reduce_fusion.14), channel_id=1, replica_groups=mesh['groups'=2,'pts'=4,'cam'=4] {'cam'}, dimensions={1}, use_global_device_ids=true | all-gather | bytes 61440 | tf_op jit(solution)/shard_map/all_gather | solution.py:134
  183.6 1.1 fusion.36
  184.9 19.0 %psum.75 = f32[9,512]{1,0:T(8,128)S(1)} all-reduce(f32[9,512]{1,0:T(8,128)S(1)} %reshape.970), channel_id=1, replica_groups=mesh['groups'=2,'pts'=4,'cam'=4] {'pts'}, use_global_device_ids=true, to_apply=%region_32.33 | all-reduce | flops 4608 | bytes 36864 | tf_op jit(solution)/shard_map/psum | solution.py:136
  204.5 6.6 %psum.76 = f32[]{:T(128)} all-reduce(f32[]{:T(128)} %multiply_reduce_fusion.18), channel_id=1, replica_groups=mesh['groups'=2,'pts'=4,'cam'=4] {'cam'}, use_global_device_ids=true, to_apply=%region_34.35 | all-reduce | flops 1 | bytes 8 | tf_op jit(solution)/shard_map/psum | solution.py:139
  213.0 6.6 %psum.77 = f32[]{:T(128)} all-reduce(f32[]{:T(128)} %get-tuple-element.12), channel_id=1, replica_groups=mesh['groups'=2,'pts'=4,'cam'=4] {'cam'}, use_global_device_ids=true, to_apply=%region_36.37 | all-reduce | flops 1 | bytes 8 | tf_op jit(solution)/shard_map/psum | solution.py:107
  223.0 1.4 fusion.18
  224.4 2.9 copy.109
  227.4 29.1 %reduce-scatter.17.cloned.1.call-done = f32[1024,3]{1,0:T(8,128)} async-done(((f32[4096,3]{1,0:T(8,128)}), f32[1024,3]{1,0:T(8,128)}) %reduce-scatter.17.cloned.1.call-update) | async-done | bytes 12304
  256.5 1.2 copy.106
  257.8 5.2 %all_gather.11 = f32[3,4096]{1,0:T(4,128)S(1)} all-gather(f32[3,1024]{1,0:T(4,128)S(1)} %multiply_reduce_fusion.13), channel_id=1, replica_groups=mesh['groups'=2,'pts'=4,'cam'=4] {'cam'}, dimensions={1}, use_global_device_ids=true | all-gather | bytes 61440 | tf_op jit(solution)/shard_map/all_gather | solution.py:134
  265.3 1.1 fusion.42
  266.6 19.0 %psum.78 = f32[9,512]{1,0:T(8,128)S(1)} all-reduce(f32[9,512]{1,0:T(8,128)S(1)} %reshape.980), channel_id=1, replica_groups=mesh['groups'=2,'pts'=4,'cam'=4] {'pts'}, use_global_device_ids=true, to_apply=%region_45.46 | all-reduce | flops 4608 | bytes 36864 | tf_op jit(solution)/shard_map/psum | solution.py:136
  286.2 6.6 %psum.79 = f32[]{:T(128)} all-reduce(f32[]{:T(128)} %multiply_reduce_fusion.16), channel_id=1, replica_groups=mesh['groups'=2,'pts'=4,'cam'=4] {'cam'}, use_global_device_ids=true, to_apply=%region_47.48 | all-reduce | flops 1 | bytes 8 | tf_op jit(solution)/shard_map/psum | solution.py:139
  (119 shorter events, 25.1 us)
Async XLA Ops:
  7.2 62.4 %reduce-scatter.13.cloned.1.call-start = ((), (), s32[]{:S(2)}) async-start(), calls=%async_computation.5 | async-start | bytes 2621440
  10.6 22.2 %copy-start.2 = (f32[9,512]{1,0:T(8,128)S(1)}, f32[9,512]{1,0:T(8,128)}, u32[]{:S(2)}) copy-start(f32[9,512]{1,0:T(8,128)} %param.13) | copy-start | bytes 55300
  10.6 22.2 %copy-start.3 = (f32[512]{0:T(512)S(1)}, f32[512]{0:T(512)}, u32[]{:S(2)}) copy-start(f32[512]{0:T(512)} %param.12) | copy-start | bytes 6148
  33.6 1.0 copy-start
  33.7 1.1 copy-start.1
  40.0 51.6 %reduce-scatter.11.cloned.1.call-start = ((), (), s32[]{:S(2)}) async-start(), calls=%async_computation.4 | async-start | bytes 163840 | tf_op jit(solution)/shard_map/reduce_scatter | solution.py:118
  45.4 129.4 %reduce-scatter.15.cloned.1.call-start = ((), (), s32[]{:S(2)}) async-start(), calls=%async_computation.6 | async-start | bytes 2621440
  145.7 110.8 %reduce-scatter.17.cloned.1.call-start = ((), (), s32[]{:S(2)}) async-start(), calls=%async_computation.7 | async-start | bytes 2621440
Sparse Core Ops, SparseCore 0:
  40.2 29.3 reduce-scatter.12
  72.0 19.6 reduce-scatter.10
  145.8 28.8 reduce-scatter.14
  227.5 28.9 reduce-scatter.16
where the time goes:
time: 302 us; the launch traced here: 301 us
  blocking collectives  126 us (42%)
  waiting for transfers between devices  102 us (34%)
  between operations  21.1 us (7%)
  local copies, waits for them, and re-layouts  19.2 us (6%)
  other arithmetic  16.9 us (6%)
  matrix products  15 us (5%)
    unnamed x7, waiting for transfers between devices  81.6 us
    psum x3, blocking collectives, on_device(): lax.psum(by_cam.segsum(jnp.sum(cam_jac * z[:, None, :], axis=0)), 'pts')  56.9 us
    reduce_scatter x1, waiting for transfers between devices, on_device(): lax.psum_scatter(six_terms, 'cam', scatter_dimension=1, tiled=True)  20.9 us
    psum x1, blocking collectives, on_device(): cam_diag = lax.psum(diag_terms, 'pts') + cam_damp[None, :]  20.9 us
    psum x3, blocking collectives, norm_sum(): return lax.psum(value, 'cam')  19.5 us
    all_gather x3, blocking collectives, on_device(): w = lax.all_gather(w_share, 'cam', axis=1, tiled=True)  15.9 us
    psum x2, blocking collectives, on_device(): alpha = rz / lax.psum(jnp.sum(direction * image), 'cam')  13.1 us
    unnamed x14, local copies, waits for them, and re-layouts  13 us
  transfers between devices with their start and end apart: 4, of which 4 were waited for; matrix products, arithmetic and copies ran while one was open for 2% of the time, Pallas kernels for 0%

commit v1 on v0

--- a/solution.py
+++ b/solution.py
@@ -133,8 +133,8 @@
         w_share = jnp.sum(inv_share * u_share[None, :, :], axis=1)
         w = lax.all_gather(w_share, "cam", axis=1, tiled=True)
         z = y - jnp.sum(point_jac * by_point.gather(w)[None], axis=1)
-        image = cam_damp[None, :] * direction + lax.psum(
-            by_cam.segsum(jnp.sum(cam_jac * z[:, None, :], axis=0)), "pts"
+        image = cam_damp[None, :] * direction + jnp.sum(
+            lax.all_gather(by_cam.segsum(jnp.sum(cam_jac * z[:, None, :], axis=0)), "pts"), axis=0
         )
         alpha = rz / lax.psum(jnp.sum(direction * image), "cam")
         solution = solution + alpha * direction

time: 302 us -> 291 us (0.964)
  blocking collectives: 126 us -> 110 us
  waiting for transfers between devices: 102 us -> 108 us
    psum x3 -> x0, blocking collectives: 56.9 us -> none  [on_device(): lax.psum(by_cam.segsum(jnp.sum(cam_jac * z[:, None, :], axis=0)), 'pts')]
    all_gather x0 -> x3, blocking collectives: none -> 40.5 us  [on_device(): lax.all_gather(by_cam.segsum(jnp.sum(cam_jac * z[:, None, :], axis=0)), '...]
    unnamed x7, waiting for transfers between devices: 81.6 us -> 87.3 us
where the time goes in v1:
time: 291 us; the launch traced here: 290 us
  blocking collectives  110 us (38%)
  waiting for transfers between devices  108 us (37%)
  between operations  21.1 us (7%)
  local copies, waits for them, and re-layouts  19.2 us (7%)
  other arithmetic  17 us (6%)
  matrix products  15 us (5%)
    unnamed x7, waiting for transfers between devices  87.3 us
    all_gather x3, blocking collectives, on_device(): lax.all_gather(by_cam.segsum(jnp.sum(cam_jac * z[:, None, :], axis=0)), '...  40.5 us
    reduce_scatter x1, waiting for transfers between devices, on_device(): lax.psum_scatter(six_terms, 'cam', scatter_dimension=1, tiled=True)  20.9 us
    psum x1, blocking collectives, on_device(): cam_diag = lax.psum(diag_terms, 'pts') + cam_damp[None, :]  20.8 us
    psum x3, blocking collectives, norm_sum(): return lax.psum(value, 'cam')  19.5 us
    all_gather x3, blocking collectives, on_device(): w = lax.all_gather(w_share, 'cam', axis=1, tiled=True)  15.9 us
    psum x2, blocking collectives, on_device(): alpha = rz / lax.psum(jnp.sum(direction * image), 'cam')  13.1 us
    unnamed x14, local copies, waits for them, and re-layouts  13 us
  transfers between devices with their start and end apart: 4, of which 4 were waited for; matrix products, arithmetic and copies ran while one was open for 2% of the time, Pallas kernels for 0%

profile of v1, /device:TPU:0, one launch (start us, length us, event | category | flops | bytes accessed | tf_op | source)
XLA Modules:
  0.0 290.4 jit_solution(11457569639600192446)
XLA Ops:
  8.7 1.4 multiply_reduce_fusion.6
  10.7 1.1 fusion.24
  12.0 20.8 %psum.49 = f32[9,512]{1,0:T(8,128)S(1)} all-reduce(f32[9,512]{1,0:T(8,128)S(1)} %reshape.939), channel_id=1, replica_groups=mesh['groups'=2,'pts'=4,'cam'=4] {'pts'}, use_global_device_ids=true, to_apply=%region_1.2 | all-reduce | flops 4608 | bytes 36864 | tf_op jit(solution)/shard_map/psum | solution.py:122
  35.6 1.4 fusion.6
  37.0 2.9 %copy.104 = f32[3,64,64]{0,2,1:T(8,128)} copy(f32[3,64,64]{1,2,0:T(8,128)S(1)} %bitcast.189) | data formatting | bytes 98304
  40.5 0.9 broadcast_select_fusion.2
  41.4 3.0 %fusion = f32[64,384]{1,0:T(8,128)S(1)} fusion(bf16[384,4096]{1,0:T(8,128)(2,1)S(1)} %bitcast.157, bf16[384,4096]{1,0:T(8,128)(2,1)S(1)} %bitcast.156, bf16[384,4096]{1,0:T(8,128)(2,1)S(1)} %bitcast.155, bf16[64,4096]{1,0:T(8,128)(2,1)S(1)} %get-tuple-element.105), kind=kOutput, calls=%fused_computation | convolution fusion | flops 637009920 | bytes 10059776 | tf_op jit(solution)/shard_map/dot_general | solution.py:48
  46.1 23.5 %reduce-scatter.13.cloned.1.call-done = f32[1024,3]{1,0:T(8,128)} async-done(((f32[4096,3]{1,0:T(8,128)}), f32[1024,3]{1,0:T(8,128)}) %reduce-scatter.13.cloned.1.call-update) | async-done | bytes 12304
  69.5 1.2 copy.99
  70.8 20.9 %reduce-scatter.11.cloned.1.call-done = f32[6,1024]{1,0:T(8,128)} async-done(((f32[6,4096]{1,0:T(8,128)}), f32[6,1024]{1,0:T(8,128)}) %reduce-scatter.11.cloned.1.call-update) | async-done | bytes 24592 | tf_op jit(solution)/shard_map/reduce_scatter | solution.py:118
  94.4 5.4 %all_gather.18 = f32[3,4096]{1,0:T(4,128)S(1)} all-gather(f32[3,1024]{1,0:T(4,128)S(1)} %get-tuple-element.16), channel_id=1, replica_groups=mesh['groups'=2,'pts'=4,'cam'=4] {'cam'}, dimensions={1}, use_global_device_ids=true | all-gather | bytes 61440 | tf_op jit(solution)/shard_map/all_gather | solution.py:134
  102.1 1.1 fusion.30
  103.4 13.5 %all_gather.19 = f32[4,9,512]{2,1,0:T(8,128)S(1)} all-gather(f32[1,9,512]{2,1,0:T(8,128)S(1)} %all_gather_reshape.9), channel_id=1, replica_groups=mesh['groups'=2,'pts'=4,'cam'=4] {'pts'}, dimensions={0}, use_global_device_ids=true | all-gather | bytes 92160 | tf_op jit(solution)/shard_map/all_gather | solution.py:137
  117.6 6.6 %all-reduce = (f32[]{:T(128)}, f32[]{:T(128)}) all-reduce(f32[]{:T(128)} %get-tuple-element.9, f32[]{:T(128)} %get-tuple-element.8), channel_id=1, replica_groups=mesh['groups'=2,'pts'=4,'cam'=4] {'cam'}, use_global_device_ids=true, to_apply=%region_3.4 | all-reduce | flops 2 | bytes 16 | tf_op jit(solution)/shard_map/psum | solution.py:107
  126.1 6.4 %psum.52 = f32[]{:T(128)} all-reduce(f32[]{:T(128)} %get-tuple-element.14), channel_id=1, replica_groups=mesh['groups'=2,'pts'=4,'cam'=4] {'cam'}, use_global_device_ids=true, to_apply=%region_23.24 | all-reduce | flops 1 | bytes 8 | tf_op jit(solution)/shard_map/psum | solution.py:107
  135.8 1.4 fusion.12
  137.3 2.9 %copy.105 = f32[3,64,64]{0,2,1:T(8,128)} copy(f32[3,64,64]{1,2,0:T(8,128)S(1)} %bitcast.190) | data formatting | bytes 98304
  140.3 31.8 %reduce-scatter.15.cloned.1.call-done = f32[1024,3]{1,0:T(8,128)} async-done(((f32[4096,3]{1,0:T(8,128)}), f32[1024,3]{1,0:T(8,128)}) %reduce-scatter.15.cloned.1.call-update) | async-done | bytes 12304
  172.1 1.2 copy.101
  173.4 5.2 %all_gather.20 = f32[3,4096]{1,0:T(4,128)S(1)} all-gather(f32[3,1024]{1,0:T(4,128)S(1)} %multiply_reduce_fusion.14), channel_id=1, replica_groups=mesh['groups'=2,'pts'=4,'cam'=4] {'cam'}, dimensions={1}, use_global_device_ids=true | all-gather | bytes 61440 | tf_op jit(solution)/shard_map/all_gather | solution.py:134
  180.9 1.1 fusion.36
  182.2 13.5 %all_gather.21 = f32[4,9,512]{2,1,0:T(8,128)S(1)} all-gather(f32[1,9,512]{2,1,0:T(8,128)S(1)} %all_gather_reshape.10), channel_id=1, replica_groups=mesh['groups'=2,'pts'=4,'cam'=4] {'pts'}, dimensions={0}, use_global_device_ids=true | all-gather | bytes 92160 | tf_op jit(solution)/shard_map/all_gather | solution.py:137
  196.3 6.6 %psum.53 = f32[]{:T(128)} all-reduce(f32[]{:T(128)} %multiply_reduce_fusion.18), channel_id=1, replica_groups=mesh['groups'=2,'pts'=4,'cam'=4] {'cam'}, use_global_device_ids=true, to_apply=%region_34.35 | all-reduce | flops 1 | bytes 8 | tf_op jit(solution)/shard_map/psum | solution.py:139
  204.8 6.6 %psum.54 = f32[]{:T(128)} all-reduce(f32[]{:T(128)} %get-tuple-element.12), channel_id=1, replica_groups=mesh['groups'=2,'pts'=4,'cam'=4] {'cam'}, use_global_device_ids=true, to_apply=%region_36.37 | all-reduce | flops 1 | bytes 8 | tf_op jit(solution)/shard_map/psum | solution.py:107
  214.8 1.4 fusion.18
  216.3 2.9 %copy.106 = f32[3,64,64]{0,2,1:T(8,128)} copy(f32[3,64,64]{1,2,0:T(8,128)S(1)} %bitcast.191) | data formatting | bytes 98304
  219.2 31.9 %reduce-scatter.17.cloned.1.call-done = f32[1024,3]{1,0:T(8,128)} async-done(((f32[4096,3]{1,0:T(8,128)}), f32[1024,3]{1,0:T(8,128)}) %reduce-scatter.17.cloned.1.call-update) | async-done | bytes 12304
  251.2 1.2 copy.103
  252.4 5.2 %all_gather.22 = f32[3,4096]{1,0:T(4,128)S(1)} all-gather(f32[3,1024]{1,0:T(4,128)S(1)} %multiply_reduce_fusion.13), channel_id=1, replica_groups=mesh['groups'=2,'pts'=4,'cam'=4] {'cam'}, dimensions={1}, use_global_device_ids=true | all-gather | bytes 61440 | tf_op jit(solution)/shard_map/all_gather | solution.py:134
  259.9 1.1 fusion.42
  261.2 13.5 %all_gather.23 = f32[4,9,512]{2,1,0:T(8,128)S(1)} all-gather(f32[1,9,512]{2,1,0:T(8,128)S(1)} %all_gather_reshape.11), channel_id=1, replica_groups=mesh['groups'=2,'pts'=4,'cam'=4] {'pts'}, dimensions={0}, use_global_device_ids=true | all-gather | bytes 92160 | tf_op jit(solution)/shard_map/all_gather | solution.py:137
  275.4 6.6 %psum.55 = f32[]{:T(128)} all-reduce(f32[]{:T(128)} %multiply_reduce_fusion.16), channel_id=1, replica_groups=mesh['groups'=2,'pts'=4,'cam'=4] {'cam'}, use_global_device_ids=true, to_apply=%region_47.48 | all-reduce | flops 1 | bytes 8 | tf_op jit(solution)/shard_map/psum | solution.py:139
  (122 shorter events, 25.1 us)
Async XLA Ops:
  7.2 62.4 %reduce-scatter.13.cloned.1.call-start = ((), (), s32[]{:S(2)}) async-start(), calls=%async_computation.5 | async-start | bytes 2621440
  10.6 22.2 %copy-start.2 = (f32[9,512]{1,0:T(8,128)S(1)}, f32[9,512]{1,0:T(8,128)}, u32[]{:S(2)}) copy-start(f32[9,512]{1,0:T(8,128)} %param.13) | copy-start | bytes 55300
  10.6 22.2 %copy-start.3 = (f32[512]{0:T(512)S(1)}, f32[512]{0:T(512)}, u32[]{:S(2)}) copy-start(f32[512]{0:T(512)} %param.12) | copy-start | bytes 6148
  33.6 1.0 copy-start
  33.6 1.1 copy-start.1
  40.0 51.6 %reduce-scatter.11.cloned.1.call-start = ((), (), s32[]{:S(2)}) async-start(), calls=%async_computation.4 | async-start | bytes 163840 | tf_op jit(solution)/shard_map/reduce_scatter | solution.py:118
  45.3 126.8 %reduce-scatter.15.cloned.1.call-start = ((), (), s32[]{:S(2)}) async-start(), calls=%async_computation.6 | async-start | bytes 2621440
  140.2 110.9 %reduce-scatter.17.cloned.1.call-start = ((), (), s32[]{:S(2)}) async-start(), calls=%async_computation.7 | async-start | bytes 2621440
Sparse Core Ops, SparseCore 0:
  40.1 29.3 reduce-scatter.12
  72.0 19.6 reduce-scatter.10
  140.4 31.6 reduce-scatter.14
  219.3 31.7 reduce-scatter.16
